TPU v7x, 512 devices: a whole 4x4x16 slice. The times are simulated.
512 devices in a mesh: dp: 64 (over y, z), tensor: 8 (over x, core).
Axes of the slice: x: 4, y: 4, z: 16, core: 2. Of those that a mesh axis runs over, the one named last changes fastest.
Arguments:
- tokens: bfloat16 [65536, 1408], P(('dp', 'tensor')), may hold values from -6 to 6
- ln1_gain: float32 [1408], replicated, may hold values from 0.1 to 1.9
- ln1_shift: float32 [1408], replicated, may hold values from -3 to 3
- w_qkv: bfloat16 [1408, 16, 264], P(None, 'tensor')
- w_out: bfloat16 [16, 88, 1408], P('tensor'), may hold values from -0.625 to 0.625
- ln2_gain: float32 [1408], replicated, may hold values from 0.1 to 1.9
- ln2_shift: float32 [1408], replicated, may hold values from -3 to 3
- w_proj: bfloat16 [5632, 3584], P('dp', 'tensor'), may hold values from -0.078125 to 0.078125
- proj_bias: float32 [3584], P('tensor'), may hold values from -3 to 3
- segments: int32 [64, 256], P('dp'), may hold values from 0 to 7, never falling along the last dimension, each value on 1 to 128 neighbouring positions
- owners: int32 [16384, 1], P('dp'), may hold values from 0 to 63; in each aligned block of 256 rows (0 to 255, 256 to 511, ...) at most 8 rows name the same one
Outputs:
- delivered: bfloat16 [32768, 3584], P('dp', 'tensor')
Inputs may be any that keep to these rules, and one draw needn't show every extreme that they name: `segments`: within a pack numbers never fall, every image has 1 to 128 groups and one has exactly that many. `owners`: among the 256 merged tokens of one pack no owner gets more than 8; in some pack an owner gets exactly 8.
All inputs are finite; a program needn't handle non-finite values.
Results may differ from a plain program's by a relative error of at most 0.015.
Values may be sent and summed in bfloat16 or wider, within the bound.
No kernel may reach another device: no remote copies, remote signals or barrier semaphores. Data moves between devices by JAX's collectives and lax.ppermute only.
A program may use at most 64 MiB of HBM per device.

v0:
```python
import jax
import jax.numpy as jnp
from jax import lax
from jax.sharding import PartitionSpec as P


def layer_norm(values, gain, shift):
    wide = values.astype(jnp.float32)
    average = jnp.mean(wide, axis=-1, keepdims=True)
    centred = wide - average
    variance = jnp.mean(centred * centred, axis=-1, keepdims=True)
    return centred * lax.rsqrt(variance + 1e-06) * gain + shift


def attend(heads_qkv, token_segs):
    row_count = heads_qkv.shape[0]
    width = heads_qkv.shape[2] // 3
    queries = heads_qkv[:, :, :width]
    keys_all = heads_qkv[:, :, width : 2 * width]
    values_all = heads_qkv[:, :, 2 * width :]
    score_scale = 1.0 / jnp.sqrt(jnp.float32(width))
    block_rows = min(512, row_count)
    outputs = []
    for block_index in range(row_count // block_rows):
        lower = block_index * block_rows
        scores = (
            jnp.einsum(
                "qhd,khd->hqk",
                queries[lower : lower + block_rows],
                keys_all,
                preferred_element_type=jnp.float32,
            )
            * score_scale
        )
        same = token_segs[lower : lower + block_rows][:, None] == token_segs[None, :]
        scores = jnp.where(same[None], scores, -jnp.inf)
        row_max = jnp.max(scores, axis=-1, keepdims=True)
        exponent = jnp.exp(scores - row_max)
        probs = (exponent / jnp.sum(exponent, axis=-1, keepdims=True)).astype(jnp.bfloat16)
        context = jnp.einsum("hqk,khd->qhd", probs, values_all, preferred_element_type=jnp.float32)
        outputs.append(context.astype(jnp.bfloat16))
    return jnp.concatenate(outputs, axis=0)


def shards(
    tokens,
    ln1_gain,
    ln1_shift,
    w_qkv,
    w_out,
    ln2_gain,
    ln2_shift,
    w_proj,
    proj_bias,
    segments,
    owners,
):
    dp_count = lax.axis_size("dp")
    gathered = lax.all_gather(tokens, "tensor", axis=0, tiled=True)
    row_count = gathered.shape[0]
    normed = layer_norm(gathered, ln1_gain, ln1_shift).astype(jnp.bfloat16)
    heads_here = w_qkv.shape[1]
    heads_qkv = jnp.dot(
        normed, w_qkv.reshape(w_qkv.shape[0], -1), preferred_element_type=jnp.float32
    )
    heads_qkv = heads_qkv.astype(jnp.bfloat16).reshape(row_count, heads_here, -1)
    token_segs = jnp.repeat(segments[0], 4)
    context = attend(heads_qkv, token_segs).reshape(row_count, -1)
    out_flat = w_out.reshape(-1, w_out.shape[2])
    attn_all = lax.psum(
        jnp.dot(context, out_flat, preferred_element_type=jnp.float32).astype(jnp.bfloat16),
        "tensor",
    ).astype(jnp.float32)
    hidden = (gathered.astype(jnp.float32) + attn_all).astype(jnp.bfloat16)
    normed_all = layer_norm(hidden, ln2_gain, ln2_shift).astype(jnp.bfloat16)
    groups = row_count // 4
    merged = normed_all.reshape(groups, -1)
    summed = jnp.dot(
        merged, lax.all_gather(w_proj, "dp", axis=0, tiled=True), preferred_element_type=jnp.float32
    )
    projected = (summed + proj_bias).astype(jnp.bfloat16)
    dests = owners[:, 0]
    onehot = (dests[:, None] == jnp.arange(dp_count, dtype=jnp.int32)[None, :]).astype(jnp.int32)
    earlier = jnp.cumsum(onehot, axis=0) - onehot
    position = jnp.sum(earlier * onehot, axis=1)
    capacity = 2 * groups // dp_count
    slot_index = dests * capacity + position
    scatter_table = (
        slot_index[None, :] == jnp.arange(dp_count * capacity, dtype=jnp.int32)[:, None]
    ).astype(jnp.bfloat16)
    outgoing = jnp.dot(scatter_table, projected, preferred_element_type=jnp.float32).astype(
        jnp.bfloat16
    )
    outgoing = outgoing.reshape(dp_count, capacity, -1)
    arrived = lax.all_to_all(outgoing, "dp", split_axis=0, concat_axis=0, tiled=True)
    return arrived.reshape(dp_count * capacity, -1)


def solution(mesh):
    return jax.shard_map(
        shards,
        mesh=mesh,
        in_specs=(
            P(("dp", "tensor"), None),
            P(),
            P(),
            P(None, "tensor", None),
            P("tensor", None, None),
            P(),
            P(),
            P("dp", "tensor"),
            P("tensor"),
            P("dp", None),
            P("dp", None),
        ),
        out_specs=P("dp", "tensor"),
        check_vma=False,
    )
```

profile of v0, /device:TPU:8, one launch (start us, length us, event | category | flops | bytes accessed | tf_op | source)
XLA Modules:
  0.0 273.7 jit_solution(15908829058235544437)
XLA Ops:
  7.4 0.0 copy-start
  7.4 0.0 all-gather.3.cloned.1.call-start
  7.4 0.7 all-gather.3.cloned.1.call-update
  8.1 0.0 all-reduce.2.cloned.1.call-start
  8.1 0.7 slice_bitcast_fusion.1
  8.8 0.1 broadcast_in_dim.24
  8.9 0.1 eq.84
  9.0 0.1 broadcast_in_dim.28
  9.1 0.1 eq.89
  9.2 0.8 broadcast_in_dim.25
  10.0 0.1 eq.86
  10.1 0.7 broadcast_compare_fusion.1
  10.8 38.3 %all-gather.3.cloned.1.call-done = bf16[1024,1408]{1,0:T(8,128)(2,1)} async-done(((bf16[128,1408]{1,0:T(8,128)(2,1)}), bf16[1024,1408]{1,0:T(8,128)(2,1)}) %all-gather.3.cloned.1.call-update) | async-done | bytes 2883600 | tf_op jit(solution)/shard_map/all_gather | solution.py:59
  49.1 2.4 convert_reduce_fusion
  51.5 0.3 copy-done.1
  51.7 0.9 fusion.6
  52.6 0.0 copy-done
  52.7 0.0 copy-done.9
  52.7 0.0 copy-done.8
  52.7 3.1 %fusion.31 = bf16[1024,528]{0,1:T(8,128)(2,1)} fusion(bf16[1408,528]{0,1:T(8,128)(2,1)S(1)} %bitcast.40, bf16[1024,1408]{1,0:T(8,128)(2,1)S(1)} %copy-done.1, f32[1408]{0:T(1024)S(1)} %copy-done.8, f32[1408]{0:T(1024)S(1)} %copy-done.9, f32[1024]{0:T(1024)S(1)} %add_rsqrt_fusion.1, f32[1024]{0:T(1024)S(1)} %broadcast_multiply_fusion.1), kind=kOutput, calls=%fused_computation.42 | convolution fusion | flops 1531723776 | bytes 5471232 | tf_op jit(solution)/shard_map/dot_general | solution.py:63
  55.8 4.8 %fusion.90 = (f32[2,512]{1,0:T(2,128)S(1)}, f32[2,512,1024]{2,1,0:T(8,128)}) fusion(pred[512,1024]{1,0:T(8,128)(4,1)S(1)} %get-tuple-element.5, bf16[1024,2,264]{0,2,1:T(8,128)(2,1)} %bitcast.47), kind=kOutput, calls=%fused_computation.94 | convolution fusion | flops 188744704 | bytes 5263360 | tf_op jit(solution)/shard_map/sub | solution.py:38
  60.6 4.9 %fusion.81 = (f32[2,512]{1,0:T(2,128)S(1)}, f32[2,512,1024]{2,1,0:T(8,128)}) fusion(pred[512,1024]{1,0:T(8,128)(4,1)S(1)} %get-tuple-element.6, bf16[1024,2,264]{0,2,1:T(8,128)(2,1)} %bitcast.48), kind=kOutput, calls=%fused_computation.93 | convolution fusion | flops 188744704 | bytes 5263360 | tf_op jit(solution)/shard_map/sub | solution.py:38
  65.4 0.0 copy-done.11
  65.4 3.2 %fusion.37 = bf16[512,2,88]{0,2,1:T(8,128)(2,1)S(1)} fusion(f32[2,512,1024]{2,1,0:T(8,128)} %get-tuple-element.12, f32[2,512]{1,0:T(2,128)S(1)} %get-tuple-element.11, bf16[1024,2,264]{0,2,1:T(8,128)(2,1)S(1)} %bitcast.49), kind=kOutput, calls=%fused_computation.48 | convolution fusion | flops 186736640 | bytes 4739072 | tf_op jit(solution)/shard_map/hqk,khd->qhd/dot_general | solution.py:40
  68.6 0.3 copy-done.12
  68.9 0.9 fusion.38
  69.7 0.2 copy-done.4
  69.9 2.7 bitcast_convert_fusion
  72.6 0.0 all-reduce.2.cloned.1.call-update
  72.6 0.2 all-gather.5.cloned.1.call-start
  72.8 0.3 all-gather.5.cloned.1.call-update
  73.2 0.6 reduce-window.6
  73.8 0.2 slice_reduce_fusion
  74.0 0.1 fusion.74
  74.2 83.9 %all-reduce.2.cloned.1.call-done = bf16[1024,1408]{1,0:T(8,128)(2,1)} async-done(((bf16[1024,1408]{1,0:T(8,128)(2,1)}), bf16[1024,1408]{1,0:T(8,128)(2,1)}) %all-reduce.2.cloned.1.call-update) | async-done | bytes 2883600 | tf_op jit(solution)/shard_map/psum | solution.py:70
  158.0 3.6 %convert_reduce_fusion.1 = f32[1024]{0:T(1024)S(1)} fusion(bf16[1024,1408]{1,0:T(8,128)(2,1)} %all-reduce.2.cloned.1.call-done, bf16[1024,1408]{1,0:T(8,128)(2,1)} %all-gather.3.cloned.1.call-done), kind=kLoop, calls=%fused_computation.6 | loop fusion | flops 8649728 | bytes 5771264 | tf_op jit(solution)/shard_map/reduce_sum | solution.py:9
  161.7 0.0 copy-start.6
  161.7 0.0 copy-start.7
  161.7 0.7 copy-done.3
  162.4 1.2 fusion.10
  163.7 2.9 %fusion.13 = bf16[1024,1408]{1,0:T(8,128)(2,1)} fusion(f32[1408]{0:T(1024)S(1)} %copy-done.6, f32[1408]{0:T(1024)S(1)} %copy-done.7, f32[1024]{0:T(1024)S(1)} %add_rsqrt_fusion, f32[1024]{0:T(1024)S(1)} %broadcast_multiply_fusion, bf16[1024,1408]{1,0:T(8,128)(2,1)S(1)} %copy-done.3, bf16[1024,1408]{1,0:T(8,128)(2,1)S(1)} %copy-done.2), kind=kLoop, calls=%fused_computation.18 | loop fusion | flops 14417920 | bytes 8670208 | tf_op jit(solution)/shard_map/convert_element_type | solution.py:75
  166.5 5.7 %reshape.149 = bf16[256,5632]{1,0:T(8,128)(2,1)} reshape(bf16[1024,1408]{1,0:T(8,128)(2,1)} %fusion.13) | data formatting | bytes 5767168 | tf_op jit(solution)/shard_map/reshape | solution.py:77
  172.2 54.6 %all-gather.5.cloned.1.call-done = bf16[5632,448]{1,0:T(8,128)(2,1)} async-done(((bf16[88,448]{1,0:T(8,128)(2,1)}), bf16[5632,448]{1,0:T(8,128)(2,1)}) %all-gather.5.cloned.1.call-update) | async-done | bytes 5046288 | tf_op jit(solution)/shard_map/all_gather | solution.py:79
  226.8 0.0 copy-done.10
  226.8 5.5 %convolution_convert_fusion = bf16[512,448]{0,1:T(8,128)(2,1)S(1)} fusion(bf16[256,5632]{1,0:T(8,128)(2,1)} %reshape.149, bf16[5632,448]{1,0:T(8,128)(2,1)} %all-gather.5.cloned.1.call-done, f32[448]{0:T(512)S(1)} %copy-done.10, s32[256]{0:T(256)S(1)} %multiply_add_fusion), kind=kOutput, calls=%fused_computation.43 | convolution fusion | flops 1409875968 | bytes 8391424 | tf_op jit(solution)/shard_map/dot_general | solution.py:91
  232.2 0.2 copy.13
  232.4 32.8 %all_to_all.5 = bf16[64,8,448]{2,1,0:T(8,128)(2,1)S(1)} all-to-all(bf16[64,8,448]{2,1,0:T(8,128)(2,1)S(1)} %bitcast.41), channel_id=1, replica_groups=mesh['dp'=64,'tensor'=8] {'dp'}, dimensions={0} | all-to-all | bytes 917504 | tf_op jit(solution)/shard_map/all_to_all | solution.py:95
  265.3 1.0 copy.14
  (22 shorter events, 0.1 us)
Async XLA Ops:
  7.4 45.3 %copy-start = (bf16[1408,2,264]{0,2,1:T(8,128)(2,1)S(1)}, bf16[1408,2,264]{0,2,1:T(8,128)(2,1)}, u32[]{:S(2)}) copy-start(bf16[1408,2,264]{0,2,1:T(8,128)(2,1)} %param.14) | copy-start | bytes 4460548
  7.4 45.3 %copy-start.9 = (f32[1408]{0:T(1024)S(1)}, f32[1408]{0:T(1024)}, u32[]{:S(2)}) copy-start(f32[1408]{0:T(1024)} %param.12) | copy-start | bytes 16900
  7.4 45.3 %copy-start.8 = (f32[1408]{0:T(1024)S(1)}, f32[1408]{0:T(1024)}, u32[]{:S(2)}) copy-start(f32[1408]{0:T(1024)} %param.13) | copy-start | bytes 16900
  7.4 41.7 %all-gather.3.cloned.1.call-start = ((), (), s32[]{:S(2)}) async-start(), calls=%async_computation.1 | async-start | bytes 3244032 | tf_op jit(solution)/shard_map/all_gather | solution.py:59
  8.1 149.9 %all-reduce.2.cloned.1.call-start = ((), (), s32[]{:S(2)}) async-start(), calls=%async_computation.2 | async-start | bytes 5767168 | tf_op jit(solution)/shard_map/psum | solution.py:70
  49.1 2.7 copy-start.1
  60.6 4.9 %copy-start.11 = (bf16[1024,528]{0,1:T(8,128)(2,1)S(1)}, bf16[1024,528]{0,1:T(8,128)(2,1)}, u32[]{:S(2)}) copy-start(bf16[1024,528]{0,1:T(8,128)(2,1)} %fusion.31) | copy-start | bytes 3244036
  65.4 3.4 %copy-start.12 = (f32[2,512,1024]{2,1,0:T(8,128)S(1)}, f32[2,512,1024]{2,1,0:T(8,128)}, u32[]{:S(2)}) copy-start(f32[2,512,1024]{2,1,0:T(8,128)} %get-tuple-element.10) | copy-start | bytes 12582916
  68.9 1.0 copy-start.4
  69.9 3.3 %copy-start.5 = (s32[256,1]{0,1:T(1,128)S(1)}, s32[256,1]{0,1:T(1,128)}, u32[]{:S(2)}) copy-start(s32[256,1]{0,1:T(1,128)} %param.21) | copy-start | bytes 3076
  72.6 154.1 %all-gather.5.cloned.1.call-start = ((), (), s32[]{:S(2)}) async-start(), calls=%async_computation.3 | async-start | bytes 5857280 | tf_op jit(solution)/shard_map/all_gather | solution.py:79
  158.0 3.7 %copy-start.2 = (bf16[1024,1408]{1,0:T(8,128)(2,1)S(1)}, bf16[1024,1408]{1,0:T(8,128)(2,1)}, u32[]{:S(2)}) copy-start(bf16[1024,1408]{1,0:T(8,128)(2,1)} %all-gather.3.cloned.1.call-done) | copy-start | bytes 8650756
  158.0 4.4 %copy-start.3 = (bf16[1024,1408]{1,0:T(8,128)(2,1)S(1)}, bf16[1024,1408]{1,0:T(8,128)(2,1)}, u32[]{:S(2)}) copy-start(bf16[1024,1408]{1,0:T(8,128)(2,1)} %all-reduce.2.cloned.1.call-done) | copy-start | bytes 8650756
  161.7 2.0 copy-start.6
  161.7 2.0 copy-start.7
  166.5 60.2 %copy-start.10 = (f32[448]{0:T(512)S(1)}, f32[448]{0:T(512)}, u32[]{:S(2)}) copy-start(f32[448]{0:T(512)} %param.19) | copy-start | bytes 5380
Sparse Core Ops, SparseCore 0:
  10.3 38.6 all-gather.2
  72.7 85.2 all-reduce.1
Sparse Core Ops, SparseCore 1:
  76.0 150.7 all-gather.4
where the time goes:
time: 274 us
  waiting for transfers between devices  178 us (65%)
  blocking collectives  32.8 us (12%)
  matrix products  24.9 us (9%)
  between operations  15 us (5%)
  other arithmetic  12.5 us (5%)
  local copies, waits for them, and re-layouts  10.4 us (4%)
    psum x1, waiting for transfers between devices, shards(): lax.psum(jnp.dot(context, out_flat, preferred_element_type=jnp.float32).a...  83.9 us
    all_gather x1, waiting for transfers between devices, shards(): lax.all_gather(w_proj, 'dp', axis=0, tiled=True)  54.6 us
    all_gather x1, waiting for transfers between devices, shards(): gathered = lax.all_gather(tokens, 'tensor', axis=0, tiled=True)  38.3 us
    all_to_all x1, blocking collectives, shards(): lax.all_to_all(outgoing, 'dp', split_axis=0, concat_axis=0, tiled=True)  32.8 us
    sub x2, matrix products, attend(): exponent = jnp.exp(scores - row_max)  9.63 us
    reduce_sum x2, other arithmetic, layer_norm(): average = jnp.mean(wide, axis=-1, keepdims=True)  6.05 us
    reshape x1, local copies, waits for them, and re-layouts, shards(): merged = normed_all.reshape(groups, -1)  5.67 us
  transfers between devices with their start and end apart: 3, of which 3 were waited for; matrix products, arithmetic and copies ran while one was open for 6% of the time, Pallas kernels for 0%

commit v1 on v0

--- a/solution.py
+++ b/solution.py
@@ -56,7 +56,9 @@
     owners,
 ):
     dp_count = lax.axis_size("dp")
-    gathered = lax.all_gather(tokens, "tensor", axis=0, tiled=True)
+    gathered = jnp.concatenate(
+        lax.all_to_all(jnp.stack([tokens] * lax.axis_size("tensor")), "tensor", 0, 0), axis=0
+    )
     row_count = gathered.shape[0]
     normed = layer_norm(gathered, ln1_gain, ln1_shift).astype(jnp.bfloat16)
     heads_here = w_qkv.shape[1]

time: 274 us -> 282 us (1.029)
  the two profiles are of different devices: /device:TPU:8 before, /device:TPU:6 now
where the time goes in v1:
time: 282 us; the launch traced here: 281 us
  waiting for transfers between devices  168 us (60%)
  blocking collectives  31.5 us (11%)
  matrix products  24.7 us (9%)
  other arithmetic  20.4 us (7%)
  between operations  15 us (5%)
  local copies, waits for them, and re-layouts  11 us (4%)
  starting transfers between devices  10.4 us (4%)
    psum x1, waiting for transfers between devices, shards(): lax.psum(jnp.dot(context, out_flat, preferred_element_type=jnp.float32).a...  79.1 us
    all_gather x1, waiting for transfers between devices, shards(): lax.all_gather(w_proj, 'dp', axis=0, tiled=True)  56.2 us
    all_to_all x1, waiting for transfers between devices, shards(): lax.all_to_all(jnp.stack([tokens] * lax.axis_size('tensor')), 'tensor', 0...  32.3 us
    all_to_all x1, blocking collectives, shards(): lax.all_to_all(outgoing, 'dp', split_axis=0, concat_axis=0, tiled=True)  31.5 us
    all_to_all x1, starting transfers between devices, shards(): lax.all_to_all(jnp.stack([tokens] * lax.axis_size('tensor')), 'tensor', 0...  10.2 us
    sub x2, matrix products, attend(): exponent = jnp.exp(scores - row_max)  9.63 us
    reduce_sum x2, other arithmetic, layer_norm(): average = jnp.mean(wide, axis=-1, keepdims=True)  5.9 us
    reduce_sum x2, other arithmetic, layer_norm(): variance = jnp.mean(centred * centred, axis=-1, keepdims=True)  5.84 us
  transfers between devices with their start and end apart: 3, of which 3 were waited for; matrix products, arithmetic and copies ran while one was open for 7% of the time, Pallas kernels for 0%

profile of v1, /device:TPU:6, one launch (start us, length us, event | category | flops | bytes accessed | tf_op | source)
XLA Modules:
  0.0 281.1 jit_solution(12066228646879942163)
XLA Ops:
  7.4 0.0 copy-start
  7.4 2.9 %stack.2 = bf16[8,128,1408]{2,1,0:T(8,128)(2,1)} broadcast(bf16[128,1408]{1,0:T(8,128)(2,1)} %param.11), dimensions={1,2} | broadcast | bytes 3244032 | tf_op jit(solution)/shard_map/stack | solution.py:60
  10.3 10.2 %all-to-all-start = ((bf16[8,128,1408]{2,1,0:T(8,128)(2,1)}), bf16[8,128,1408]{2,1,0:T(8,128)(2,1)}, u32[]{:S(2)}, u32[]{:S(2)}) async-start(bf16[8,128,1408]{2,1,0:T(8,128)(2,1)} %stack.2), calls=%async_computation | async-start | bytes 5767168 | tf_op jit(solution)/shard_map/all_to_all | solution.py:60
  20.5 0.0 all-reduce.2.cloned.1.call-start
  20.5 0.0 copy-done.8
  20.6 0.1 broadcast_in_dim.24
  20.6 0.1 eq.84
  20.8 0.1 broadcast_in_dim.28
  20.8 0.1 eq.89
  20.9 0.1 broadcast_in_dim.25
  21.0 0.1 eq.86
  21.2 0.7 broadcast_compare_fusion.1
  21.8 32.3 %all-to-all-done = bf16[8,128,1408]{2,1,0:T(8,128)(2,1)} async-done(((bf16[8,128,1408]{2,1,0:T(8,128)(2,1)}), bf16[8,128,1408]{2,1,0:T(8,128)(2,1)}, u32[]{:S(2)}, u32[]{:S(2)}) %all-to-all-start) | async-done | bytes 2883616 | tf_op jit(solution)/shard_map/all_to_all | solution.py:60
  54.1 2.3 convert_reduce_fusion.1
  56.4 2.7 multiply_reduce_fusion
  59.1 0.0 copy-done.4
  59.1 0.0 copy-done.5
  59.1 2.9 %add_convert_fusion = bf16[8,128,1408]{2,1,0:T(8,128)(2,1)S(1)} fusion(bf16[8,128,1408]{2,1,0:T(8,128)(2,1)} %all-to-all-done, f32[1408]{0:T(1024)S(1)} %copy-done.4, f32[1408]{0:T(1024)S(1)} %copy-done.5, f32[8,128]{1,0:T(8,128)S(1)} %add_rsqrt_fusion.1, f32[8,128]{1,0:T(8,128)S(1)} %broadcast_multiply_fusion.1), kind=kLoop, calls=%fused_computation.13 | loop fusion | flops 8650752 | bytes 5786624 | tf_op jit(solution)/shard_map/convert_element_type | solution.py:63
  62.1 0.0 copy-done
  62.1 2.9 %convolution_convert_fusion = bf16[1024,528]{0,1:T(8,128)(2,1)} fusion(bf16[1024,1408]{1,0:T(8,128)(2,1)S(1)} %bitcast.53, bf16[1408,528]{0,1:T(8,128)(2,1)S(1)} %bitcast.52), kind=kOutput, calls=%fused_computation.32 | convolution fusion | flops 1523073024 | bytes 5451776 | tf_op jit(solution)/shard_map/dot_general | solution.py:65
  65.0 4.8 %fusion.75 = (f32[2,512]{1,0:T(2,128)S(1)}, f32[2,512,1024]{2,1,0:T(8,128)}) fusion(pred[512,1024]{1,0:T(8,128)(4,1)S(1)} %get-tuple-element.5, bf16[1024,2,264]{0,2,1:T(8,128)(2,1)} %bitcast.60), kind=kOutput, calls=%fused_computation.84 | convolution fusion | flops 188744704 | bytes 5263360 | tf_op jit(solution)/shard_map/sub | solution.py:38
  69.7 4.9 %fusion.66 = (f32[2,512]{1,0:T(2,128)S(1)}, f32[2,512,1024]{2,1,0:T(8,128)}) fusion(pred[512,1024]{1,0:T(8,128)(4,1)S(1)} %get-tuple-element.6, bf16[1024,2,264]{0,2,1:T(8,128)(2,1)} %bitcast.61), kind=kOutput, calls=%fused_computation.83 | convolution fusion | flops 188744704 | bytes 5263360 | tf_op jit(solution)/shard_map/sub | solution.py:38
  74.6 0.0 copy-done.10
  74.6 3.2 %fusion.22 = bf16[512,2,88]{0,2,1:T(8,128)(2,1)S(1)} fusion(f32[2,512,1024]{2,1,0:T(8,128)} %get-tuple-element.12, f32[2,512]{1,0:T(2,128)S(1)} %get-tuple-element.11, bf16[1024,2,264]{0,2,1:T(8,128)(2,1)S(1)} %bitcast.62), kind=kOutput, calls=%fused_computation.38 | convolution fusion | flops 186736640 | bytes 4739072 | tf_op jit(solution)/shard_map/hqk,khd->qhd/dot_general | solution.py:40
  77.8 0.2 copy-done.11
  78.1 0.9 fusion.23
  78.9 0.2 copy-done.2
  79.1 2.7 bitcast_convert_fusion
  81.8 0.0 all-reduce.2.cloned.1.call-update
  81.8 0.2 all-gather.2.cloned.1.call-start
  82.0 0.3 all-gather.2.cloned.1.call-update
  82.4 0.0 copy-done.3
  82.4 0.6 reduce-window.6
  83.0 0.2 slice_reduce_fusion
  83.2 0.1 fusion.59
  83.4 79.1 %all-reduce.2.cloned.1.call-done = bf16[1024,1408]{1,0:T(8,128)(2,1)} async-done(((bf16[1024,1408]{1,0:T(8,128)(2,1)}), bf16[1024,1408]{1,0:T(8,128)(2,1)}) %all-reduce.2.cloned.1.call-update) | async-done | bytes 2883600 | tf_op jit(solution)/shard_map/psum | solution.py:72
  162.4 3.6 %convert_reduce_fusion = f32[1024]{0:T(1024)S(1)} fusion(bf16[1024,1408]{1,0:T(8,128)(2,1)} %all-reduce.2.cloned.1.call-done, bf16[8,128,1408]{2,1,0:T(8,128)(2,1)} %all-to-all-done), kind=kLoop, calls=%fused_computation.3 | loop fusion | flops 8649728 | bytes 5771264 | tf_op jit(solution)/shard_map/reduce_sum | solution.py:9
  166.1 0.0 copy-start.6
  166.1 0.0 copy-start.7
  166.1 0.0 copy-done.1
  166.1 3.1 %fusion.4 = f32[1024]{0:T(1024)S(1)} fusion(f32[1024]{0:T(1024)S(1)} %broadcast_multiply_fusion, bf16[1024,1408]{1,0:T(8,128)(2,1)S(1)} %copy-done.1, bf16[8,128,1408]{2,1,0:T(8,128)(2,1)} %all-to-all-done), kind=kLoop, calls=%fused_computation.6 | loop fusion | flops 11533312 | bytes 5775360 | tf_op jit(solution)/shard_map/reduce_sum | solution.py:11
  169.3 4.3 %fusion.7 = bf16[1024,1408]{1,0:T(8,128)(2,1)} fusion(f32[1408]{0:T(1024)S(1)} %copy-done.6, f32[1408]{0:T(1024)S(1)} %copy-done.7, f32[1024]{0:T(1024)S(1)} %add_rsqrt_fusion, f32[1024]{0:T(1024)S(1)} %broadcast_multiply_fusion, bf16[1024,1408]{1,0:T(8,128)(2,1)S(1)} %copy-done.1, bf16[8,128,1408]{2,1,0:T(8,128)(2,1)} %all-to-all-done), kind=kLoop, calls=%fused_computation.9 | loop fusion | flops 14417920 | bytes 8670208 | tf_op jit(solution)/shard_map/convert_element_type | solution.py:77
  173.6 5.6 %reshape.186 = bf16[256,5632]{1,0:T(8,128)(2,1)} reshape(bf16[1024,1408]{1,0:T(8,128)(2,1)} %fusion.7) | data formatting | bytes 5767168 | tf_op jit(solution)/shard_map/reshape | solution.py:79
  179.2 56.2 %all-gather.2.cloned.1.call-done = bf16[5632,448]{1,0:T(8,128)(2,1)} async-done(((bf16[88,448]{1,0:T(8,128)(2,1)}), bf16[5632,448]{1,0:T(8,128)(2,1)}) %all-gather.2.cloned.1.call-update) | async-done | bytes 5046288 | tf_op jit(solution)/shard_map/all_gather | solution.py:81
  235.5 5.5 %convolution_convert_fusion.1 = bf16[512,448]{0,1:T(8,128)(2,1)S(1)} fusion(bf16[256,5632]{1,0:T(8,128)(2,1)} %reshape.186, bf16[5632,448]{1,0:T(8,128)(2,1)} %all-gather.2.cloned.1.call-done, f32[448]{0:T(512)S(1)} %copy-done.9, s32[256]{0:T(256)S(1)} %multiply_add_fusion), kind=kOutput, calls=%fused_computation.33 | convolution fusion | flops 1409875968 | bytes 8391424 | tf_op jit(solution)/shard_map/dot_general | solution.py:93
  240.9 0.2 copy.13
  241.1 31.5 %all_to_all.10 = bf16[64,8,448]{2,1,0:T(8,128)(2,1)S(1)} all-to-all(bf16[64,8,448]{2,1,0:T(8,128)(2,1)S(1)} %bitcast.54), channel_id=1, replica_groups=mesh['dp'=64,'tensor'=8] {'dp'}, dimensions={0} | all-to-all | bytes 917504 | tf_op jit(solution)/shard_map/all_to_all | solution.py:97
  272.7 1.0 copy.14
  (21 shorter events, 0.1 us)
Async XLA Ops:
  7.4 54.7 %copy-start = (bf16[1408,2,264]{0,2,1:T(8,128)(2,1)S(1)}, bf16[1408,2,264]{0,2,1:T(8,128)(2,1)}, u32[]{:S(2)}) copy-start(bf16[1408,2,264]{0,2,1:T(8,128)(2,1)} %param.14) | copy-start | bytes 4460548
  7.4 13.2 %copy-start.8 = (s32[1,256]{1,0:T(1,128)S(1)}, s32[1,256]{1,0:T(1,128)}, u32[]{:S(2)}) copy-start(s32[1,256]{1,0:T(1,128)} %param.20) | copy-start | bytes 3076
  10.3 43.8 %all-to-all-start = ((bf16[8,128,1408]{2,1,0:T(8,128)(2,1)}), bf16[8,128,1408]{2,1,0:T(8,128)(2,1)}, u32[]{:S(2)}, u32[]{:S(2)}) async-start(bf16[8,128,1408]{2,1,0:T(8,128)(2,1)} %stack.2), calls=%async_computation | async-start | bytes 5767168 | tf_op jit(solution)/shard_map/all_to_all | solution.py:60
  20.5 38.6 %copy-start.4 = (f32[1408]{0:T(1024)S(1)}, f32[1408]{0:T(1024)}, u32[]{:S(2)}) copy-start(f32[1408]{0:T(1024)} %param.13) | copy-start | bytes 16900
  20.5 38.6 %copy-start.5 = (f32[1408]{0:T(1024)S(1)}, f32[1408]{0:T(1024)}, u32[]{:S(2)}) copy-start(f32[1408]{0:T(1024)} %param.12) | copy-start | bytes 16900
  20.5 141.9 %all-reduce.2.cloned.1.call-start = ((), (), s32[]{:S(2)}) async-start(), calls=%async_computation.2 | async-start | bytes 5767168 | tf_op jit(solution)/shard_map/psum | solution.py:72
  69.7 4.9 %copy-start.10 = (bf16[1024,528]{0,1:T(8,128)(2,1)S(1)}, bf16[1024,528]{0,1:T(8,128)(2,1)}, u32[]{:S(2)}) copy-start(bf16[1024,528]{0,1:T(8,128)(2,1)} %convolution_convert_fusion) | copy-start | bytes 3244036
  74.6 3.4 %copy-start.11 = (f32[2,512,1024]{2,1,0:T(8,128)S(1)}, f32[2,512,1024]{2,1,0:T(8,128)}, u32[]{:S(2)}) copy-start(f32[2,512,1024]{2,1,0:T(8,128)} %get-tuple-element.10) | copy-start | bytes 12582916
  78.1 1.0 copy-start.2
  79.1 3.3 %copy-start.3 = (s32[256,1]{0,1:T(1,128)S(1)}, s32[256,1]{0,1:T(1,128)}, u32[]{:S(2)}) copy-start(s32[256,1]{0,1:T(1,128)} %param.21) | copy-start | bytes 3076
  81.8 153.7 %all-gather.2.cloned.1.call-start = ((), (), s32[]{:S(2)}) async-start(), calls=%async_computation.3 | async-start | bytes 5857280 | tf_op jit(solution)/shard_map/all_gather | solution.py:81
  162.4 3.7 %copy-start.1 = (bf16[1024,1408]{1,0:T(8,128)(2,1)S(1)}, bf16[1024,1408]{1,0:T(8,128)(2,1)}, u32[]{:S(2)}) copy-start(bf16[1024,1408]{1,0:T(8,128)(2,1)} %all-reduce.2.cloned.1.call-done) | copy-start | bytes 8650756
  166.1 3.2 %copy-start.6 = (f32[1408]{0:T(1024)S(1)}, f32[1408]{0:T(1024)}, u32[]{:S(2)}) copy-start(f32[1408]{0:T(1024)} %param.17) | copy-start | bytes 16900
  166.1 3.2 %copy-start.7 = (f32[1408]{0:T(1024)S(1)}, f32[1408]{0:T(1024)}, u32[]{:S(2)}) copy-start(f32[1408]{0:T(1024)} %param.16) | copy-start | bytes 16900
  173.6 61.8 %copy-start.9 = (f32[448]{0:T(512)S(1)}, f32[448]{0:T(512)}, u32[]{:S(2)}) copy-start(f32[448]{0:T(512)} %param.19) | copy-start | bytes 5380
Sparse Core Ops, SparseCore 0:
  81.9 80.4 all-reduce.1
Sparse Core Ops, SparseCore 1:
  85.2 150.2 all-gather.1
